TPU v7x, 512 devices: a whole 4x8x8 slice. The times are simulated.
512 devices in a mesh: tm: 32 (over x, y), space: 16 (over z, core).
Axes of the slice: x: 4, y: 8, z: 8, core: 2. Of those that a mesh axis runs over, the one named last changes fastest.
Arguments:
- data: bfloat16 [4096, 131072], P('tm', 'space'), may hold values from -40 to 40
- weights: float32 [131072], P('space'), may hold values from 1 to 30
- freqs: int32 [32], replicated, may hold values from 0 to 32, as said below
- n_keep: int32 [32], replicated, may hold values from 1 to 64, as said below
Outputs:
- mode_field: bfloat16 [32, 2, 64, 131072], P('tm', None, None, 'space')
- energy: float32 [32], P('tm')
Inputs may be any that keep to these rules, and one draw needn't show every extreme that they name: `freqs`: 32 distinct bins, among them 0 and 32, in an order drawn from the seed. `n_keep`: some frequency keeps all 64 columns and another keeps one.
All inputs are finite; a program needn't handle non-finite values.
Results may differ from a plain program's by a relative error of at most 0.0052.
Values may be sent and summed in bfloat16 or wider, within the bound.
No kernel may reach another device: no remote copies, remote signals or barrier semaphores. Data moves between devices by JAX's collectives and lax.ppermute only.
A program may use at most 64 MiB of HBM per device.

v0:
```python
import jax
import jax.numpy as jnp
from jax import lax
from jax.sharding import PartitionSpec as P

NT = 64
NS_STEPS = 4


def spectra_table(freqs):
    time_int = jnp.arange(NT, dtype=jnp.int32)
    time_float = time_int.astype(jnp.float32)
    window = 0.5 - 0.5 * jnp.cos(2.0 * jnp.pi * time_float / NT)
    norm = jnp.sqrt(jnp.sum(window * window))
    wrapped = freqs[:, None] * time_int[None, :] % NT
    phase_angle = 2.0 * jnp.pi * wrapped.astype(jnp.float32) / NT
    real_rows = window[None, :] * jnp.cos(phase_angle) / norm
    imag_rows = -window[None, :] * jnp.sin(phase_angle) / norm
    return jnp.concatenate([real_rows, imag_rows], axis=0).astype(jnp.bfloat16)


def transform_blocks(dft_table, snapshots, freq_count):
    block_count = snapshots.shape[0] // NT
    point_count = snapshots.shape[1]
    block_view = snapshots.reshape(block_count, NT, point_count)
    spectra = jnp.einsum("rt,btp->rbp", dft_table, block_view, preferred_element_type=jnp.float32)
    return spectra.reshape(2, freq_count, block_count, point_count)


def gram_terms(spectra, point_weights, total_points):
    spectra_re = spectra[0]
    spectra_im = spectra[1]
    stacked = jnp.concatenate([spectra_re, spectra_im], axis=1)
    square = (
        jnp.einsum(
            "fip,fjp->fij",
            stacked * point_weights[None, None, :],
            stacked,
            precision=lax.Precision.HIGHEST,
        )
        / total_points
    )
    return square


def unfold_terms(summed, block_count):
    g_one = summed[:, :block_count, :block_count] + summed[:, block_count:, block_count:]
    g_two = summed[:, :block_count, block_count:] - summed[:, block_count:, :block_count]
    return (g_one, g_two)


def inverse_root(embedded):
    size_two = embedded.shape[1]
    frobenius = jnp.sqrt(jnp.sum(embedded * embedded, axis=(1, 2)) + 1e-06)
    identity = jnp.broadcast_to(jnp.eye(size_two, dtype=jnp.float32), embedded.shape)
    current = embedded / frobenius[:, None, None]
    result = identity
    for sweep in range(NS_STEPS):
        factor = 1.5 * identity - 0.5 * jnp.einsum(
            "fij,fjk->fik", result, current, precision=lax.Precision.HIGHEST
        )
        current = jnp.einsum("fij,fjk->fik", current, factor, precision=lax.Precision.HIGHEST)
        result = jnp.einsum("fij,fjk->fik", factor, result, precision=lax.Precision.HIGHEST)
    return result


def finish_modes(spectra, summed, kept_counts, block_count):
    g_one, g_two = unfold_terms(summed, block_count)
    embedded = jnp.concatenate(
        [jnp.concatenate([g_one, -g_two], axis=2), jnp.concatenate([g_two, g_one], axis=2)], axis=1
    )
    inv_root = inverse_root(embedded)
    z_top = inv_root[:, :block_count, :block_count]
    z_low = inv_root[:, block_count:, :block_count]
    spectra_re = spectra[0]
    spectra_im = spectra[1]
    mode_re = jnp.einsum(
        "fij,fip->fjp", z_top, spectra_re, precision=lax.Precision.HIGHEST
    ) - jnp.einsum("fij,fip->fjp", z_low, spectra_im, precision=lax.Precision.HIGHEST)
    mode_im = jnp.einsum(
        "fij,fip->fjp", z_top, spectra_im, precision=lax.Precision.HIGHEST
    ) + jnp.einsum("fij,fip->fjp", z_low, spectra_re, precision=lax.Precision.HIGHEST)
    kept_mask = jnp.arange(block_count, dtype=jnp.int32)[None, :] < kept_counts[:, None]
    both_parts = jnp.stack([mode_re, mode_im], axis=1)
    mode_field = jnp.where(
        kept_mask[:, None, :, None], both_parts, jnp.zeros_like(both_parts)
    ).astype(jnp.bfloat16)
    energy = jnp.trace(g_one, axis1=1, axis2=2) / block_count
    return (mode_field, energy)


def shards(data, weights, freqs, n_keep):
    tm_count = lax.axis_size("tm")
    freq_count = freqs.shape[0]
    points_here = data.shape[1]
    total_points = points_here * lax.axis_size("space")
    block_count = data.shape[0] // NT * tm_count
    dft_table = spectra_table(freqs)
    spectra = transform_blocks(dft_table, data, freq_count)
    regrouped = lax.all_to_all(spectra, "tm", split_axis=1, concat_axis=2, tiled=True)
    partial_value = gram_terms(regrouped, weights, total_points)
    summed = lax.psum(partial_value, "space")
    kept_counts = lax.dynamic_slice_in_dim(n_keep, lax.axis_index("tm"), 1)
    mode_field, energy = finish_modes(regrouped, summed, kept_counts, block_count)
    return (mode_field, energy)


def solution(mesh):
    placed = (P("tm", "space"), P("space"), P(), P())
    return jax.shard_map(
        shards,
        mesh=mesh,
        in_specs=placed,
        out_specs=(P("tm", None, None, "space"), P("tm")),
        check_vma=False,
    )
```

profile of v0, /device:TPU:1, one launch (start us, length us, event | category | flops | bytes accessed | tf_op | source)
XLA Modules:
  0.0 300.4 jit_solution(1019790081844584022)
XLA Ops:
  7.2 0.0 copy-start
  7.2 0.7 multiply_reduce_fusion
  8.6 0.8 divide_convert_fusion.1
  9.4 0.0 copy-done
  9.4 0.7 fusion.36
  10.1 5.2 %copy.10 = f32[2,32,2,8192]{3,2,0,1:T(2,128)} copy(f32[2,32,2,8192]{3,1,2,0:T(8,128)S(1)} %fusion.36) | data formatting | bytes 8388608 | tf_op jit(solution)/shard_map/rt,btp->rbp/dot_general | solution.py:26
  15.3 0.0 copy-start.4
  15.3 10.7 %all-to-all-start = ((f32[2,32,2,8192]{3,2,0,1:T(2,128)}), f32[2,32,2,8192]{3,2,0,1:T(2,128)}, u32[]{:S(2)}, u32[]{:S(2)}) async-start(f32[2,32,2,8192]{3,2,0,1:T(2,128)} %copy.10), calls=%async_computation | async-start | bytes 8388608 | tf_op jit(solution)/shard_map/all_to_all | solution.py:100
  26.1 0.0 all-reduce.2.cloned.1.call-start
  26.1 0.0 copy-done.4
  26.1 0.6 dynamic_slice.3
  26.7 92.0 %all-to-all-done = f32[2,32,2,8192]{3,2,0,1:T(2,128)} async-done(((f32[2,32,2,8192]{3,2,0,1:T(2,128)}), f32[2,32,2,8192]{3,2,0,1:T(2,128)}, u32[]{:S(2)}, u32[]{:S(2)}) %all-to-all-start) | async-done | bytes 4194336 | tf_op jit(solution)/shard_map/all_to_all | solution.py:100
  118.7 4.8 %fusion.35 = (f32[1,32,2,8192]{3,2,0,1:T(2,128)}, f32[1,32,2,8192]{3,2,0,1:T(2,128)}) fusion(f32[2,32,2,8192]{3,2,0,1:T(2,128)} %all-to-all-done), kind=kLoop, calls=%fused_computation.61 | loop fusion | bytes 8388608 | tf_op jit(solution)/shard_map/slice | solution.py:31
  123.5 5.2 %squeeze.8 = f32[1,64,8192]{2,0,1:T(1,128)} reshape(f32[1,32,2,8192]{3,2,0,1:T(2,128)} %get-tuple-element.6) | data formatting | bytes 4194304 | tf_op jit(solution)/shard_map/squeeze | solution.py:31
  128.7 3.7 %concatenate.53 = f32[64,8192]{1,0:T(8,128)} reshape(f32[1,32,2,8192]{3,2,0,1:T(2,128)} %get-tuple-element.6) | data formatting | bytes 4194304 | tf_op jit(solution)/shard_map/concatenate | solution.py:33
  132.4 5.2 %squeeze.9 = f32[1,64,8192]{2,0,1:T(1,128)} reshape(f32[1,32,2,8192]{3,2,0,1:T(2,128)} %get-tuple-element.7) | data formatting | bytes 4194304 | tf_op jit(solution)/shard_map/squeeze | solution.py:32
  137.6 3.6 %concatenate.54 = f32[64,8192]{1,0:T(8,128)} reshape(f32[1,32,2,8192]{3,2,0,1:T(2,128)} %get-tuple-element.7) | data formatting | bytes 4194304 | tf_op jit(solution)/shard_map/concatenate | solution.py:33
  141.3 0.0 copy-start.3
  141.3 12.4 %pad_maximum_fusion = f32[1,128,8192]{2,0,1:T(1,128)} fusion(f32[1,64,8192]{2,0,1:T(1,128)} %squeeze.9, f32[1,64,8192]{2,0,1:T(1,128)} %squeeze.8), kind=kLoop, calls=%fused_computation.8 | loop fusion | flops 1048576 | bytes 8388608 | tf_op jit(solution)/shard_map/concatenate | solution.py:33
  153.6 0.0 copy-done.3
  153.6 9.6 %fusion.16 = f32[1,128,128]{2,1,0:T(8,128)} fusion(f32[1,128,8192]{2,0,1:T(1,128)} %pad_maximum_fusion, f32[64,8192]{1,0:T(8,128)} %concatenate.54, f32[64,8192]{1,0:T(8,128)} %concatenate.53, f32[8192]{0:T(1024)S(1)} %copy-done.3), kind=kOutput, calls=%fused_computation.24 | convolution fusion | flops 1612726272 | bytes 8486912 | tf_op jit(solution)/shard_map/fip,fjp->fij/dot_general | solution.py:35
  163.2 0.0 all-reduce.2.cloned.1.call-update
  163.3 0.7 iota_compare_fusion.4
  163.9 110.4 %all-reduce.2.cloned.1.call-done = f32[1,128,128]{2,1,0:T(8,128)} async-done(((f32[1,128,128]{2,1,0:T(8,128)}), f32[1,128,128]{2,1,0:T(8,128)}) %all-reduce.2.cloned.1.call-update) | async-done | bytes 65552 | tf_op jit(solution)/shard_map/psum | solution.py:102
  274.3 1.5 fusion.34
  275.9 0.7 fusion.19
  276.6 0.1 maximum_bitcast_fusion
  277.3 0.0 copy-start.1
  277.3 0.2 fusion.12
  277.5 0.2 fusion.29
  277.7 0.2 fusion.20
  277.9 0.2 fusion.11
  278.1 0.2 fusion.38
  278.3 0.2 fusion.37
  278.6 0.2 fusion.10
  278.8 0.2 fusion.40
  279.0 0.2 fusion.39
  279.2 0.2 fusion.9
  279.4 0.2 convolution_bitcast_fusion
  279.6 0.0 copy-done.1
  279.6 0.0 copy-start.2
  279.6 2.2 fusion.22
  281.8 0.0 copy-done.2
  281.8 1.9 fusion.21
  283.7 2.0 fusion.1
  285.8 3.0 %fusion = bf16[1,1,64,8192]{3,2,1,0:T(8,128)(2,1)} fusion(f32[64,8192]{1,0:T(8,128)S(1)} %fusion.21, f32[64,8192]{1,0:T(8,128)S(1)} %copy-done.1, f32[1,128,128]{2,1,0:T(8,128)S(1)} %convolution_bitcast_fusion), kind=kOutput, calls=%fused_computation.1 | convolution fusion | flops 403701760 | bytes 5275648 | tf_op jit(solution)/shard_map/fij,fip->fjp/dot_general | solution.py:82
  289.4 3.0 fusion.5
  (2 shorter events, 0.1 us)
Async XLA Ops:
  7.2 2.2 copy-start
  15.3 10.8 %copy-start.4 = (s32[32]{0:T(128)S(1)}, s32[32]{0:T(128)}, u32[]{:S(2)}) copy-start(s32[32]{0:T(128)} %param.7) | copy-start | bytes 388
  15.3 103.4 %all-to-all-start = ((f32[2,32,2,8192]{3,2,0,1:T(2,128)}), f32[2,32,2,8192]{3,2,0,1:T(2,128)}, u32[]{:S(2)}, u32[]{:S(2)}) async-start(f32[2,32,2,8192]{3,2,0,1:T(2,128)} %copy.10), calls=%async_computation | async-start | bytes 8388608 | tf_op jit(solution)/shard_map/all_to_all | solution.py:100
  26.1 248.3 %all-reduce.2.cloned.1.call-start = ((), (), s32[]{:S(2)}) async-start(), calls=%async_computation.1 | async-start | bytes 131072 | tf_op jit(solution)/shard_map/psum | solution.py:102
  141.3 12.4 %copy-start.3 = (f32[8192]{0:T(1024)S(1)}, f32[8192]{0:T(1024)}, u32[]{:S(2)}) copy-start(f32[8192]{0:T(1024)} %param.5) | copy-start | bytes 98308
  277.3 2.3 copy-start.1
  279.6 2.2 copy-start.2
Sparse Core Ops, SparseCore 0:
  163.4 110.9 all-reduce.1
where the time goes:
time: 301 us; the launch traced here: 300 us
  waiting for transfers between devices  202 us (67%)
  local copies, waits for them, and re-layouts  28.4 us (9%)
  matrix products  21.6 us (7%)
  other arithmetic  19.8 us (7%)
  between operations  17.4 us (6%)
  starting transfers between devices  10.8 us (4%)
    psum x1, waiting for transfers between devices, shards(): summed = lax.psum(partial_value, 'space')  110 us
    all_to_all x1, waiting for transfers between devices, shards(): lax.all_to_all(spectra, 'tm', split_axis=1, concat_axis=2, tiled=True)  92 us
    concatenate x1, other arithmetic, gram_terms(): stacked = jnp.concatenate([spectra_re, spectra_im], axis=1)  12.4 us
    all_to_all x1, starting transfers between devices, shards(): lax.all_to_all(spectra, 'tm', split_axis=1, concat_axis=2, tiled=True)  10.7 us
    dot_general x1, matrix products, gram_terms(): jnp.einsum('fip,fjp->fij', stacked * point_weights[None, None, :], stacke...  9.63 us
    concatenate x2, local copies, waits for them, and re-layouts, gram_terms(): stacked = jnp.concatenate([spectra_re, spectra_im], axis=1)  7.32 us
  transfers between devices with their start and end apart: 2, of which 2 were waited for; matrix products, arithmetic and copies ran while one was open for 0% of the time, Pallas kernels for 0%

commit v1 on v0

--- a/solution.py
+++ b/solution.py
@@ -99,7 +99,8 @@
     spectra = transform_blocks(dft_table, data, freq_count)
     regrouped = lax.all_to_all(spectra, "tm", split_axis=1, concat_axis=2, tiled=True)
     partial_value = gram_terms(regrouped, weights, total_points)
-    summed = lax.psum(partial_value, "space")
+    parts = lax.all_gather(partial_value, "space", axis=0, tiled=False)
+    summed = parts.sum(axis=0)
     kept_counts = lax.dynamic_slice_in_dim(n_keep, lax.axis_index("tm"), 1)
     mode_field, energy = finish_modes(regrouped, summed, kept_counts, block_count)
     return (mode_field, energy)

time: 301 us -> 231 us (0.77)
  waiting for transfers between devices: 202 us -> 45.4 us
  blocking collectives: 0 us -> 102 us
  starting transfers between devices: 10.8 us -> 0.04 us
  local copies, waits for them, and re-layouts: 28.4 us -> 24 us
    psum x1 -> x0, waiting for transfers between devices: 110 us -> none  [shards(): summed = lax.psum(partial_value, 'space')]
    all_to_all x0 -> x1, blocking collectives: none -> 102 us  [shards(): lax.all_to_all(spectra, 'tm', split_axis=1, concat_axis=2, tiled=True)]
    all_to_all x1 -> x0, waiting for transfers between devices: 92 us -> none  [shards(): lax.all_to_all(spectra, 'tm', split_axis=1, concat_axis=2, tiled=True)]
    all_gather x0 -> x1, waiting for transfers between devices: none -> 45.4 us  [shards(): parts = lax.all_gather(partial_value, 'space', axis=0, tiled=False)]
    all_to_all x1 -> x0, starting transfers between devices: 10.7 us -> none  [shards(): lax.all_to_all(spectra, 'tm', split_axis=1, concat_axis=2, tiled=True)]
  transfers between devices with their start and end apart: 2 -> 1, of which waited for: 2 -> 1; matrix products, arithmetic and copies ran while one was open for 0% -> 1% of each run, Pallas kernels for 0% -> 0%
where the time goes in v1:
time: 231 us
  blocking collectives  102 us (44%)
  waiting for transfers between devices  45.4 us (20%)
  local copies, waits for them, and re-layouts  24 us (10%)
  matrix products  21.7 us (9%)
  other arithmetic  20.3 us (9%)
  between operations  17.4 us (8%)
    all_to_all x1, blocking collectives, shards(): lax.all_to_all(spectra, 'tm', split_axis=1, concat_axis=2, tiled=True)  102 us
    all_gather x1, waiting for transfers between devices, shards(): parts = lax.all_gather(partial_value, 'space', axis=0, tiled=False)  45.4 us
    concatenate x1, other arithmetic, gram_terms(): stacked = jnp.concatenate([spectra_re, spectra_im], axis=1)  12.3 us
    dot_general x1, matrix products, gram_terms(): jnp.einsum('fip,fjp->fij', stacked * point_weights[None, None, :], stacke...  9.63 us
    concatenate x2, local copies, waits for them, and re-layouts, gram_terms(): stacked = jnp.concatenate([spectra_re, spectra_im], axis=1)  7.33 us
    squeeze x1, local copies, waits for them, and re-layouts, gram_terms(): spectra_re = spectra[0]  5.26 us
    squeeze x1, local copies, waits for them, and re-layouts, gram_terms(): spectra_im = spectra[1]  5.23 us
  transfers between devices with their start and end apart: 1, of which 1 were waited for; matrix products, arithmetic and copies ran while one was open for 1% of the time, Pallas kernels for 0%

profile of v1, /device:TPU:1, one launch (start us, length us, event | category | flops | bytes accessed | tf_op | source)
XLA Modules:
  0.0 230.9 jit_solution(18289746690409185046)
XLA Ops:
  7.2 0.0 copy-start
  7.2 0.0 all-gather.3.cloned.1.call-start
  7.3 0.7 multiply_reduce_fusion
  8.6 0.8 divide_convert_fusion.1
  9.4 0.0 copy-done
  9.5 0.7 fusion.33
  10.1 3.2 %copy.11 = f32[2,32,2,8192]{3,2,0,1:T(2,128)S(1)} copy(f32[2,32,2,8192]{3,1,2,0:T(8,128)S(1)} %fusion.33) | data formatting | bytes 8388608 | tf_op jit(solution)/shard_map/rt,btp->rbp/dot_general | solution.py:26
  13.4 102.2 %all_to_all.4 = f32[2,32,2,8192]{3,2,0,1:T(2,128)S(1)} all-to-all(f32[2,32,2,8192]{3,2,0,1:T(2,128)S(1)} %copy.11), channel_id=1, replica_groups=mesh['tm'=32,'space'=16] {'tm'}, dimensions={1} | all-to-all | bytes 8388608 | tf_op jit(solution)/shard_map/all_to_all | solution.py:100
  115.6 2.3 fusion.32
  117.9 5.3 %squeeze.8 = f32[1,64,8192]{2,0,1:T(1,128)} reshape(f32[1,32,2,8192]{3,2,0,1:T(2,128)} %get-tuple-element.6) | data formatting | bytes 4194304 | tf_op jit(solution)/shard_map/squeeze | solution.py:31
  123.1 3.7 %concatenate.53 = f32[64,8192]{1,0:T(8,128)} reshape(f32[1,32,2,8192]{3,2,0,1:T(2,128)} %get-tuple-element.6) | data formatting | bytes 4194304 | tf_op jit(solution)/shard_map/concatenate | solution.py:33
  126.8 5.2 %squeeze.9 = f32[1,64,8192]{2,0,1:T(1,128)} reshape(f32[1,32,2,8192]{3,2,0,1:T(2,128)} %get-tuple-element.7) | data formatting | bytes 4194304 | tf_op jit(solution)/shard_map/squeeze | solution.py:32
  132.1 3.6 %concatenate.54 = f32[64,8192]{1,0:T(8,128)} reshape(f32[1,32,2,8192]{3,2,0,1:T(2,128)} %get-tuple-element.7) | data formatting | bytes 4194304 | tf_op jit(solution)/shard_map/concatenate | solution.py:33
  135.7 0.0 copy-start.3
  135.7 12.3 %pad_maximum_fusion = f32[1,128,8192]{2,0,1:T(1,128)} fusion(f32[1,64,8192]{2,0,1:T(1,128)} %squeeze.9, f32[1,64,8192]{2,0,1:T(1,128)} %squeeze.8), kind=kLoop, calls=%fused_computation.8 | loop fusion | flops 1048576 | bytes 8388608 | tf_op jit(solution)/shard_map/concatenate | solution.py:33
  148.0 0.0 copy-done.3
  148.1 0.0 copy-start.4
  148.1 9.6 %fusion.13 = f32[128,128]{1,0:T(8,128)} fusion(f32[1,128,8192]{2,0,1:T(1,128)} %pad_maximum_fusion, f32[64,8192]{1,0:T(8,128)} %concatenate.54, f32[64,8192]{1,0:T(8,128)} %concatenate.53, f32[8192]{0:T(1024)S(1)} %copy-done.3), kind=kOutput, calls=%fused_computation.23 | convolution fusion | flops 1612726272 | bytes 8486912 | tf_op jit(solution)/shard_map/fip,fjp->fij/dot_general | solution.py:35
  157.7 0.0 all-gather.3.cloned.1.call-update
  157.7 0.0 copy-done.4
  157.7 0.6 dynamic_slice.3
  158.3 0.6 iota_compare_fusion.4
  159.0 45.4 %all-gather.3.cloned.1.call-done = f32[2048,128]{1,0:T(8,128)} async-done(((f32[128,128]{1,0:T(8,128)}), f32[2048,128]{1,0:T(8,128)}) %all-gather.3.cloned.1.call-update) | async-done | bytes 1048592 | tf_op jit(solution)/shard_map/all_gather | solution.py:102
  204.4 1.3 reduce.3
  205.6 0.7 fusion.31
  206.3 0.7 fusion.16
  207.0 0.1 maximum_bitcast_fusion
  207.8 0.0 copy-start.1
  207.8 0.2 fusion.12
  208.0 0.2 fusion.26
  208.2 0.2 fusion.17
  208.4 0.2 fusion.11
  208.6 0.2 fusion.35
  208.8 0.2 fusion.34
  209.1 0.2 fusion.10
  209.3 0.2 fusion.37
  209.5 0.2 fusion.36
  209.7 0.2 fusion.9
  209.9 0.2 convolution_bitcast_fusion
  210.1 0.0 copy-done.1
  210.1 0.0 copy-start.2
  210.1 2.2 fusion.19
  212.3 0.0 copy-done.2
  212.3 1.9 fusion.18
  214.2 2.0 fusion.1
  216.3 3.0 %fusion = bf16[1,1,64,8192]{3,2,1,0:T(8,128)(2,1)} fusion(f32[64,8192]{1,0:T(8,128)S(1)} %fusion.18, f32[64,8192]{1,0:T(8,128)S(1)} %copy-done.1, f32[1,128,128]{2,1,0:T(8,128)S(1)} %convolution_bitcast_fusion), kind=kOutput, calls=%fused_computation.1 | convolution fusion | flops 403701760 | bytes 5275648 | tf_op jit(solution)/shard_map/fij,fip->fjp/dot_general | solution.py:82
  220.0 3.0 %fusion.5 = bf16[1,2,64,8192]{3,2,1,0:T(8,128)(2,1)} fusion(bf16[1,1,64,8192]{3,2,1,0:T(8,128)(2,1)} %fusion, bf16[1,1,64,8192]{3,2,1,0:T(8,128)(2,1)S(1)} %fusion.1, pred[64]{0:T(512)(128)(4,1)S(1)} %iota_compare_fusion.4), kind=kLoop, calls=%fused_computation.10 | loop fusion | flops 5242880 | bytes 4194368 | tf_op jit(solution)/shard_map/convert_element_type | solution.py:87
  (2 shorter events, 0.1 us)
Async XLA Ops:
  7.2 2.3 copy-start
  7.2 197.2 %all-gather.3.cloned.1.call-start = ((), (), s32[]{:S(2)}) async-start(), calls=%async_computation.1 | async-start | bytes 1114112 | tf_op jit(solution)/shard_map/all_gather | solution.py:102
  135.7 12.3 %copy-start.3 = (f32[8192]{0:T(1024)S(1)}, f32[8192]{0:T(1024)}, u32[]{:S(2)}) copy-start(f32[8192]{0:T(1024)} %param.5) | copy-start | bytes 98308
  148.1 9.7 %copy-start.4 = (s32[32]{0:T(128)S(1)}, s32[32]{0:T(128)}, u32[]{:S(2)}) copy-start(s32[32]{0:T(128)} %param.7) | copy-start | bytes 388
  207.8 2.3 copy-start.1
  210.1 2.2 copy-start.2
Sparse Core Ops, SparseCore 0:
  157.8 46.4 all-gather.2
